TPU v7x, 32 devices: a whole 2x2x4 slice. The times are simulated.
32 devices in a mesh: job: 2 (over x), space: 4 (over y, core), arc: 4 (over z).
Axes of the slice: x: 2, y: 2, z: 4, core: 2. Of those that a mesh axis runs over, the one named last changes fastest.
Arguments:
- saved_velocity_trajectory: bfloat16 [64, 3, 8, 128, 128], P(('job', 'arc'), None, 'space'), parts along dimension 0, may hold values from -4 to 4
- saved_warmth_trajectory: bfloat16 [64, 8, 128, 128], P(('job', 'arc'), 'space'), parts along dimension 0, may hold values from -5 to 5
- control_porosity: float32 [16, 128, 128], P(('job', 'space')), parts along dimension 0, may hold values from 0.05 to 1
- control_volume_flag: int32 [16, 128, 128], P(('job', 'space')), parts along dimension 0, may hold values 0 or 1
- entrance_face_flag: int32 [256, 128], P('job'), parts along dimension 0, may hold values 0 or 1
Outputs:
- gradient: float32 [16, 128, 128], P(('job', 'space'), 'arc'), parts along dimension 0
- entry_adjoint: float32 [8, 4, 8, 128, 128], P(('job', 'arc'), None, 'space'), parts along dimension 0
There are 2 independent parts, one for each index of `job`. A program takes and returns all parts, laid end to end along the dimension named above; each array names one. Nothing has to cross between parts.
All inputs are finite; a program needn't handle non-finite values. No bound on the sum of `control_volume_flag` on one device may be relied on, other than what follows from the above.
Results may differ from a plain program's by a relative error of at most 0.0003.
Values may be sent and summed in bfloat16 or wider, within the bound.
No kernel may reach another device: no remote copies, remote signals or barrier semaphores. Data moves between devices by JAX's collectives and lax.ppermute only.
A program may use at most 64 MiB of HBM per device.

v0:
```python
import jax
import jax.numpy as jnp
from jax import lax
from jax.sharding import PartitionSpec as P


def padded(cells, sides, width):
    for axis, dim in sides:
        count = lax.axis_size(axis)
        ends = count - 1
        head = lax.slice_in_dim(cells, 0, width, axis=dim)
        tail = lax.slice_in_dim(cells, cells.shape[dim] - width, cells.shape[dim], axis=dim)
        cells = jnp.concatenate(
            [
                lax.ppermute(tail, axis, [(i, (i + 1) % count) for i in range(ends)]),
                cells,
                lax.ppermute(head, axis, [((i + 1) % count, i) for i in range(ends)]),
            ],
            axis=dim,
        )
    return cells


def passed_along(value, axis, steps):
    count = lax.axis_size(axis)
    pairs = [(source, (source + steps) % count) for source in range(count)]
    return lax.ppermute(value, axis, pairs)


def laplace(ext):
    mid = ext[..., 1:-1, 1:-1, 1:-1]
    total = ext[..., 2:, 1:-1, 1:-1] + ext[..., :-2, 1:-1, 1:-1]
    total = total + ext[..., 1:-1, 2:, 1:-1] + ext[..., 1:-1, :-2, 1:-1]
    total = total + ext[..., 1:-1, 1:-1, 2:] + ext[..., 1:-1, 1:-1, :-2]
    return total - 6.0 * mid


def slopes(ext):
    return (
        0.5 * (ext[..., 2:, 1:-1, 1:-1] - ext[..., :-2, 1:-1, 1:-1]),
        0.5 * (ext[..., 1:-1, 2:, 1:-1] - ext[..., 1:-1, :-2, 1:-1]),
        0.5 * (ext[..., 1:-1, 1:-1, 2:] - ext[..., 1:-1, 1:-1, :-2]),
    )


def pad_sides(field, operating_variant):
    widths = [(0, 0)] * (field.ndim - 2) + [(1, 1), (1, 1)]
    return jnp.pad(field, widths, mode=operating_variant)


def adjoint_update(
    adj,
    ext_a,
    ext_b,
    padded_thermal_field,
    speed,
    alpha,
    porosity_sensitivity,
    solid,
    quadrature_factor,
):
    a_now = adj[:3]
    current_adjoint_vector = adj[3]
    grad_b = slopes(ext_b)
    grad_a = slopes(ext_a)
    grad_t = slopes(padded_thermal_field)
    carry_b = speed[0] * grad_b[0] + speed[1] * grad_b[1] + speed[2] * grad_b[2]
    carry_a = speed[0:1] * grad_a[0] + speed[1:2] * grad_a[1] + speed[2:3] * grad_a[2]
    thermal_current_field = padded_thermal_field[1:-1, 1:-1, 1:-1]
    grad_stack = jnp.stack(grad_t)
    new_a = a_now + 0.1 * (
        1.2 * laplace(ext_a) + carry_a - alpha * a_now - current_adjoint_vector * grad_stack
    )
    new_b = current_adjoint_vector + 0.1 * (
        1.2 * laplace(ext_b) + carry_b - 2.0 * solid * current_adjoint_vector + 2.0 * solid
    )
    common_divisor_lcm_like = jnp.sum(a_now * speed, axis=0)
    summand_contribution = (
        0.1
        * quadrature_factor
        * (
            porosity_sensitivity * common_divisor_lcm_like
            + 2.0 * (current_adjoint_vector - 1.0) * thermal_current_field
        )
    )
    return (jnp.concatenate([new_a, new_b[None]], axis=0), summand_contribution)


def body(
    saved_velocity_trajectory,
    saved_warmth_trajectory,
    control_porosity,
    control_volume_flag,
    entrance_face_flag,
):
    quadrature_factor = control_volume_flag.astype(jnp.float32)
    gamma = jnp.where(control_volume_flag == 1, control_porosity, jnp.float32(0.0))
    solid = 1.0 - gamma
    alpha = 3.0 * 0.1 * solid / (0.1 + gamma)
    porosity_sensitivity = -3.0 * 0.1 * 1.1 / ((0.1 + gamma) * (0.1 + gamma))
    leading_plane = lax.axis_index("space") == 0
    trailing_plane = lax.axis_index("space") == lax.axis_size("space") - 1
    device_instant_total = saved_warmth_trajectory.shape[0]
    cycle_ext = padded(saved_warmth_trajectory, (("space", 1),), 1)

    def closing_thermal_value(thermal_current_field, with_halo_padding):
        floor_limit = jnp.where(leading_plane, thermal_current_field[0], with_halo_padding[0])
        ceiling_bound = jnp.where(trailing_plane, thermal_current_field[-1], with_halo_padding[-1])
        return pad_sides(
            jnp.concatenate(
                [floor_limit[None], thermal_current_field, ceiling_bound[None]], axis=0
            ),
            "edge",
        )

    def one_step(adj, interior_block):
        speed = saved_velocity_trajectory[interior_block].astype(jnp.float32)
        thermal_current_field = saved_warmth_trajectory[interior_block].astype(jnp.float32)
        with_halo_padding = padded(adj, (("space", 1),), 1)
        thermal_halo_values = cycle_ext[interior_block].astype(jnp.float32)
        complete_thermal_field = jnp.concatenate(
            [thermal_halo_values[:1], thermal_current_field, thermal_halo_values[-1:]], axis=0
        )
        padded_thermal_field = closing_thermal_value(thermal_current_field, complete_thermal_field)
        ext_a = pad_sides(with_halo_padding[:3], "constant")
        current_adjoint_vector = adj[3]
        floor_limit = jnp.where(
            leading_plane,
            jnp.where(entrance_face_flag == 1, jnp.float32(0.0), current_adjoint_vector[0]),
            with_halo_padding[3, 0],
        )
        ceiling_bound = jnp.where(
            trailing_plane, current_adjoint_vector[-1], with_halo_padding[3, -1]
        )
        ext_b = pad_sides(
            jnp.concatenate(
                [floor_limit[None], current_adjoint_vector, ceiling_bound[None]], axis=0
            ),
            "edge",
        )
        return adjoint_update(
            adj,
            ext_a,
            ext_b,
            padded_thermal_field,
            speed,
            alpha,
            porosity_sensitivity,
            solid,
            quadrature_factor,
        )

    grid_shape = (4,) + control_porosity.shape
    adj = jnp.zeros(grid_shape, jnp.float32)
    for interior_block in range(device_instant_total - 1, -1, -1):
        adj, unused = one_step(adj, interior_block)
    adj = passed_along(adj, "arc", -1)
    partial_sum = jnp.zeros(control_porosity.shape, jnp.float32)
    for interior_block in range(device_instant_total - 1, -1, -1):
        adj, summand_contribution = one_step(adj, interior_block)
        partial_sum = partial_sum + summand_contribution
    summed = lax.psum(partial_sum, "arc")
    share = summed.shape[1] // lax.axis_size("arc")
    gradient = lax.dynamic_slice_in_dim(summed, lax.axis_index("arc") * share, share, 1)
    return (gradient, adj[None])


def solution(mesh):
    return jax.shard_map(
        body,
        mesh=mesh,
        in_specs=(
            P(("job", "arc"), None, "space", None, None),
            P(("job", "arc"), "space", None, None),
            P(("job", "space"), None, None),
            P(("job", "space"), None, None),
            P("job", None),
        ),
        out_specs=(P(("job", "space"), "arc", None), P(("job", "arc"), None, "space", None, None)),
        check_vma=False,
    )
```

profile of v0, /device:TPU:0, one launch (start us, length us, event | category | flops | bytes accessed | tf_op | source)
XLA Modules:
  0.0 265.9 jit_solution(15857158346192255144)
XLA Ops:
  9.4 3.8 %collective-permute-start.1 = (f32[4,1,128,128]{3,2,1,0:T(8,128)}, f32[4,1,128,128]{3,2,1,0:T(8,128)}, u32[]{:S(2)}, u32[]{:S(2)}) collective-permute-start(f32[4,1,128,128]{3,2,1,0:T(8,128)} %broadcast.302), channel_id=1, source_target_pairs={{0,4},{4,8},{8,12},{1,5},{5,9},{9,13},{2,6},{6,10},{10,14},{3,7},{... | collective-permute-start | bytes 786440 | tf_op jit(solution)/shard_map/ppermute | solution.py:15
  13.1 1.9 fusion.209
  15.0 4.5 %collective-permute-start.2 = (bf16[8,1,128,128]{3,2,1,0:T(8,128)(2,1)}, bf16[8,1,128,128]{3,2,1,0:T(8,128)(2,1)}, u32[]{:S(2)}, u32[]{:S(2)}) collective-permute-start(bf16[8,1,128,128]{3,2,1,0:T(8,128)(2,1)} %get-tuple-element.84), channel_id=1, source_target_pairs={{0,4},{4,8},{8,12},{1,5},{5,9},{9,13},{2,6},{6,10},{10,14},{3,7},{... | collective-permute-start | bytes 786440 | tf_op jit(solution)/shard_map/ppermute | solution.py:15
  41.1 3.7 %collective-permute-start.5 = (f32[4,1,128,128]{3,2,1,0:T(8,128)S(1)}, f32[4,1,128,128]{3,2,1,0:T(8,128)S(1)}, u32[]{:S(2)}, u32[]{:S(2)}) collective-permute-start(f32[4,1,128,128]{3,2,1,0:T(8,128)S(1)} %get-tuple-element.81), channel_id=1, source_target_pairs={{0,4},{4,8},{8,12},{1,5},{5,9},{9,13},{2,6},{6,10},{10,14},{3,7},{... | collective-permute-start | bytes 786440 | tf_op jit(solution)/shard_map/ppermute | solution.py:15
  49.5 6.4 %collective-permute-start.7 = (f32[4,1,128,128]{3,2,1,0:T(8,128)S(1)}, f32[4,1,128,128]{3,2,1,0:T(8,128)S(1)}, u32[]{:S(2)}, u32[]{:S(2)}) collective-permute-start(f32[4,1,128,128]{3,2,1,0:T(8,128)S(1)} %get-tuple-element.79), channel_id=1, source_target_pairs={{0,4},{4,8},{8,12},{1,5},{5,9},{9,13},{2,6},{6,10},{10,14},{3,7},{... | collective-permute-start | bytes 786440 | tf_op jit(solution)/shard_map/ppermute | solution.py:15
  59.1 6.6 %collective-permute-start.9 = (f32[4,1,128,128]{3,2,1,0:T(8,128)S(1)}, f32[4,1,128,128]{3,2,1,0:T(8,128)S(1)}, u32[]{:S(2)}, u32[]{:S(2)}) collective-permute-start(f32[4,1,128,128]{3,2,1,0:T(8,128)S(1)} %get-tuple-element.77), channel_id=1, source_target_pairs={{0,4},{4,8},{8,12},{1,5},{5,9},{9,13},{2,6},{6,10},{10,14},{3,7},{... | collective-permute-start | bytes 786440 | tf_op jit(solution)/shard_map/ppermute | solution.py:15
  67.3 3.9 %collective-permute-done.8 = f32[4,1,128,128]{3,2,1,0:T(8,128)S(1)} collective-permute-done((f32[4,1,128,128]{3,2,1,0:T(8,128)S(1)}, f32[4,1,128,128]{3,2,1,0:T(8,128)S(1)}, u32[]{:S(2)}, u32[]{:S(2)}) %collective-permute-start.8) | collective-permute-done | bytes 262176 | tf_op jit(solution)/shard_map/ppermute | solution.py:17
  73.2 6.7 %collective-permute-start.11 = (f32[4,1,128,128]{3,2,1,0:T(8,128)S(1)}, f32[4,1,128,128]{3,2,1,0:T(8,128)S(1)}, u32[]{:S(2)}, u32[]{:S(2)}) collective-permute-start(f32[4,1,128,128]{3,2,1,0:T(8,128)S(1)} %get-tuple-element.75), channel_id=1, source_target_pairs={{0,4},{4,8},{8,12},{1,5},{5,9},{9,13},{2,6},{6,10},{10,14},{3,7},{... | collective-permute-start | bytes 786440 | tf_op jit(solution)/shard_map/ppermute | solution.py:15
  81.6 1.9 collective-permute-done.10
  85.6 6.4 %collective-permute-start.13 = (f32[4,1,128,128]{3,2,1,0:T(8,128)S(1)}, f32[4,1,128,128]{3,2,1,0:T(8,128)S(1)}, u32[]{:S(2)}, u32[]{:S(2)}) collective-permute-start(f32[4,1,128,128]{3,2,1,0:T(8,128)S(1)} %get-tuple-element.73), channel_id=1, source_target_pairs={{0,4},{4,8},{8,12},{1,5},{5,9},{9,13},{2,6},{6,10},{10,14},{3,7},{... | collective-permute-start | bytes 786440 | tf_op jit(solution)/shard_map/ppermute | solution.py:15
  93.6 1.9 collective-permute-done.12
  97.5 6.2 %collective-permute-start.15 = (f32[4,1,128,128]{3,2,1,0:T(8,128)S(1)}, f32[4,1,128,128]{3,2,1,0:T(8,128)S(1)}, u32[]{:S(2)}, u32[]{:S(2)}) collective-permute-start(f32[4,1,128,128]{3,2,1,0:T(8,128)S(1)} %get-tuple-element.71), channel_id=1, source_target_pairs={{0,4},{4,8},{8,12},{1,5},{5,9},{9,13},{2,6},{6,10},{10,14},{3,7},{... | collective-permute-start | bytes 786440 | tf_op jit(solution)/shard_map/ppermute | solution.py:15
  105.3 1.9 collective-permute-done.14
  109.2 6.2 %collective-permute-start.17 = (f32[4,1,128,128]{3,2,1,0:T(8,128)S(1)}, f32[4,1,128,128]{3,2,1,0:T(8,128)S(1)}, u32[]{:S(2)}, u32[]{:S(2)}) collective-permute-start(f32[4,1,128,128]{3,2,1,0:T(8,128)S(1)} %get-tuple-element.69), channel_id=1, source_target_pairs={{0,4},{4,8},{8,12},{1,5},{5,9},{9,13},{2,6},{6,10},{10,14},{3,7},{... | collective-permute-start | bytes 786440 | tf_op jit(solution)/shard_map/ppermute | solution.py:15
  117.2 1.9 collective-permute-done.16
  121.1 3.7 %collective-permute-start.18 = (f32[4,2,128,128]{3,2,1,0:T(8,128)S(1)}, f32[4,2,128,128]{3,2,1,0:T(8,128)S(1)}, u32[]{:S(2)}, u32[]{:S(2)}) collective-permute-start(f32[4,2,128,128]{3,2,1,0:T(8,128)S(1)} %pad_maximum_fusion.2), channel_id=1, source_target_pairs={{0,3},{1,0},{2,1},{3,2},{4,7},{5,4},{6,5},{7,6},{8,11},{9,8},{10,9... | collective-permute-start | bytes 1572872 | tf_op jit(solution)/shard_map/ppermute | solution.py:27
  124.8 9.0 %collective-permute-done.18 = f32[4,2,128,128]{3,2,1,0:T(8,128)S(1)} collective-permute-done((f32[4,2,128,128]{3,2,1,0:T(8,128)S(1)}, f32[4,2,128,128]{3,2,1,0:T(8,128)S(1)}, u32[]{:S(2)}, u32[]{:S(2)}) %collective-permute-start.18) | collective-permute-done | bytes 524320 | tf_op jit(solution)/shard_map/ppermute | solution.py:27
  133.8 5.3 %collective-permute-start.20 = (f32[4,1,128,128]{3,2,1,0:T(8,128)S(1)}, f32[4,1,128,128]{3,2,1,0:T(8,128)S(1)}, u32[]{:S(2)}, u32[]{:S(2)}) collective-permute-start(f32[4,1,128,128]{3,2,1,0:T(8,128)S(1)} %get-tuple-element.51), channel_id=1, source_target_pairs={{0,4},{4,8},{8,12},{1,5},{5,9},{9,13},{2,6},{6,10},{10,14},{3,7},{... | collective-permute-start | bytes 786440 | tf_op jit(solution)/shard_map/ppermute | solution.py:15
  140.5 2.1 collective-permute-done.19
  144.1 6.2 %collective-permute-start.22 = (f32[4,1,128,128]{3,2,1,0:T(8,128)S(1)}, f32[4,1,128,128]{3,2,1,0:T(8,128)S(1)}, u32[]{:S(2)}, u32[]{:S(2)}) collective-permute-start(f32[4,1,128,128]{3,2,1,0:T(8,128)S(1)} %get-tuple-element.49), channel_id=1, source_target_pairs={{0,4},{4,8},{8,12},{1,5},{5,9},{9,13},{2,6},{6,10},{10,14},{3,7},{... | collective-permute-start | bytes 786440 | tf_op jit(solution)/shard_map/ppermute | solution.py:15
  151.7 2.1 collective-permute-done.21
  155.3 6.2 %collective-permute-start.24 = (f32[4,1,128,128]{3,2,1,0:T(8,128)S(1)}, f32[4,1,128,128]{3,2,1,0:T(8,128)S(1)}, u32[]{:S(2)}, u32[]{:S(2)}) collective-permute-start(f32[4,1,128,128]{3,2,1,0:T(8,128)S(1)} %get-tuple-element.47), channel_id=1, source_target_pairs={{0,4},{4,8},{8,12},{1,5},{5,9},{9,13},{2,6},{6,10},{10,14},{3,7},{... | collective-permute-start | bytes 786440 | tf_op jit(solution)/shard_map/ppermute | solution.py:15
  162.8 2.1 collective-permute-done.23
  166.4 6.2 %collective-permute-start.26 = (f32[4,1,128,128]{3,2,1,0:T(8,128)S(1)}, f32[4,1,128,128]{3,2,1,0:T(8,128)S(1)}, u32[]{:S(2)}, u32[]{:S(2)}) collective-permute-start(f32[4,1,128,128]{3,2,1,0:T(8,128)S(1)} %get-tuple-element.45), channel_id=1, source_target_pairs={{0,4},{4,8},{8,12},{1,5},{5,9},{9,13},{2,6},{6,10},{10,14},{3,7},{... | collective-permute-start | bytes 786440 | tf_op jit(solution)/shard_map/ppermute | solution.py:15
  177.6 6.2 %collective-permute-start.28 = (f32[4,1,128,128]{3,2,1,0:T(8,128)S(1)}, f32[4,1,128,128]{3,2,1,0:T(8,128)S(1)}, u32[]{:S(2)}, u32[]{:S(2)}) collective-permute-start(f32[4,1,128,128]{3,2,1,0:T(8,128)S(1)} %get-tuple-element.43), channel_id=1, source_target_pairs={{0,4},{4,8},{8,12},{1,5},{5,9},{9,13},{2,6},{6,10},{10,14},{3,7},{... | collective-permute-start | bytes 786440 | tf_op jit(solution)/shard_map/ppermute | solution.py:15
  185.1 2.1 collective-permute-done.27
  188.7 6.2 %collective-permute-start.30 = (f32[4,1,128,128]{3,2,1,0:T(8,128)S(1)}, f32[4,1,128,128]{3,2,1,0:T(8,128)S(1)}, u32[]{:S(2)}, u32[]{:S(2)}) collective-permute-start(f32[4,1,128,128]{3,2,1,0:T(8,128)S(1)} %get-tuple-element.41), channel_id=1, source_target_pairs={{0,4},{4,8},{8,12},{1,5},{5,9},{9,13},{2,6},{6,10},{10,14},{3,7},{... | collective-permute-start | bytes 786440 | tf_op jit(solution)/shard_map/ppermute | solution.py:15
  196.2 2.1 collective-permute-done.29
  199.8 6.2 %collective-permute-start.32 = (f32[4,1,128,128]{3,2,1,0:T(8,128)S(1)}, f32[4,1,128,128]{3,2,1,0:T(8,128)S(1)}, u32[]{:S(2)}, u32[]{:S(2)}) collective-permute-start(f32[4,1,128,128]{3,2,1,0:T(8,128)S(1)} %get-tuple-element.39), channel_id=1, source_target_pairs={{0,4},{4,8},{8,12},{1,5},{5,9},{9,13},{2,6},{6,10},{10,14},{3,7},{... | collective-permute-start | bytes 786440 | tf_op jit(solution)/shard_map/ppermute | solution.py:15
  207.4 2.1 collective-permute-done.31
  213.1 6.2 %collective-permute-start.34 = (f32[4,1,128,128]{3,2,1,0:T(8,128)S(1)}, f32[4,1,128,128]{3,2,1,0:T(8,128)S(1)}, u32[]{:S(2)}, u32[]{:S(2)}) collective-permute-start(f32[4,1,128,128]{3,2,1,0:T(8,128)S(1)} %get-tuple-element.37), channel_id=1, source_target_pairs={{0,4},{4,8},{8,12},{1,5},{5,9},{9,13},{2,6},{6,10},{10,14},{3,7},{... | collective-permute-start | bytes 786440 | tf_op jit(solution)/shard_map/ppermute | solution.py:15
  220.6 34.2 %all-reduce.22.cloned.1.call-done = f32[2,128,128]{2,1,0:T(8,128)} async-done(((f32[2,128,128]{2,1,0:T(8,128)}), f32[2,128,128]{2,1,0:T(8,128)}) %all-reduce.22.cloned.1.call-update) | async-done | bytes 131088 | tf_op jit(solution)/shard_map/psum | solution.py:162
  (371 shorter events, 78.0 us)
Async XLA Ops:
  7.2 247.6 %all-reduce.22.cloned.1.call-start = ((), (), s32[]{:S(2)}) async-start(), calls=%async_computation | async-start | bytes 262144 | tf_op jit(solution)/shard_map/psum | solution.py:162
  8.0 27.7 %collective-permute-start = (f32[4,1,128,128]{3,2,1,0:T(8,128)}, f32[4,1,128,128]{3,2,1,0:T(8,128)}, u32[]{:S(2)}, u32[]{:S(2)}) collective-permute-start(f32[4,1,128,128]{3,2,1,0:T(8,128)} %broadcast.302), channel_id=1, source_target_pairs={{4,0},{8,4},{12,8},{5,1},{9,5},{13,9},{6,2},{10,6},{14,10},{7,3},{... | collective-permute-start | bytes 786440 | tf_op jit(solution)/shard_map/ppermute | solution.py:17
  9.4 25.2 %collective-permute-start.1 = (f32[4,1,128,128]{3,2,1,0:T(8,128)}, f32[4,1,128,128]{3,2,1,0:T(8,128)}, u32[]{:S(2)}, u32[]{:S(2)}) collective-permute-start(f32[4,1,128,128]{3,2,1,0:T(8,128)} %broadcast.302), channel_id=1, source_target_pairs={{0,4},{4,8},{8,12},{1,5},{5,9},{9,13},{2,6},{6,10},{10,14},{3,7},{... | collective-permute-start | bytes 786440 | tf_op jit(solution)/shard_map/ppermute | solution.py:15
  15.0 13.9 %collective-permute-start.2 = (bf16[8,1,128,128]{3,2,1,0:T(8,128)(2,1)}, bf16[8,1,128,128]{3,2,1,0:T(8,128)(2,1)}, u32[]{:S(2)}, u32[]{:S(2)}) collective-permute-start(bf16[8,1,128,128]{3,2,1,0:T(8,128)(2,1)} %get-tuple-element.84), channel_id=1, source_target_pairs={{0,4},{4,8},{8,12},{1,5},{5,9},{9,13},{2,6},{6,10},{10,14},{3,7},{... | collective-permute-start | bytes 786440 | tf_op jit(solution)/shard_map/ppermute | solution.py:15
  19.5 10.5 %collective-permute-start.3 = (bf16[8,1,128,128]{3,2,1,0:T(8,128)(2,1)}, bf16[8,1,128,128]{3,2,1,0:T(8,128)(2,1)}, u32[]{:S(2)}, u32[]{:S(2)}) collective-permute-start(bf16[8,1,128,128]{3,2,1,0:T(8,128)(2,1)} %get-tuple-element.83), channel_id=1, source_target_pairs={{4,0},{8,4},{12,8},{5,1},{9,5},{13,9},{6,2},{10,6},{14,10},{7,3},{... | collective-permute-start | bytes 786440 | tf_op jit(solution)/shard_map/ppermute | solution.py:17
  39.8 5.3 %collective-permute-start.4 = (f32[4,1,128,128]{3,2,1,0:T(8,128)S(1)}, f32[4,1,128,128]{3,2,1,0:T(8,128)S(1)}, u32[]{:S(2)}, u32[]{:S(2)}) collective-permute-start(f32[4,1,128,128]{3,2,1,0:T(8,128)S(1)} %get-tuple-element.82), channel_id=1, source_target_pairs={{4,0},{8,4},{12,8},{5,1},{9,5},{13,9},{6,2},{10,6},{14,10},{7,3},{... | collective-permute-start | bytes 786440 | tf_op jit(solution)/shard_map/ppermute | solution.py:17
  41.1 4.8 %collective-permute-start.5 = (f32[4,1,128,128]{3,2,1,0:T(8,128)S(1)}, f32[4,1,128,128]{3,2,1,0:T(8,128)S(1)}, u32[]{:S(2)}, u32[]{:S(2)}) collective-permute-start(f32[4,1,128,128]{3,2,1,0:T(8,128)S(1)} %get-tuple-element.81), channel_id=1, source_target_pairs={{0,4},{4,8},{8,12},{1,5},{5,9},{9,13},{2,6},{6,10},{10,14},{3,7},{... | collective-permute-start | bytes 786440 | tf_op jit(solution)/shard_map/ppermute | solution.py:15
  48.1 8.0 %collective-permute-start.6 = (f32[4,1,128,128]{3,2,1,0:T(8,128)S(1)}, f32[4,1,128,128]{3,2,1,0:T(8,128)S(1)}, u32[]{:S(2)}, u32[]{:S(2)}) collective-permute-start(f32[4,1,128,128]{3,2,1,0:T(8,128)S(1)} %get-tuple-element.80), channel_id=1, source_target_pairs={{4,0},{8,4},{12,8},{5,1},{9,5},{13,9},{6,2},{10,6},{14,10},{7,3},{... | collective-permute-start | bytes 786440 | tf_op jit(solution)/shard_map/ppermute | solution.py:17
  49.5 7.6 %collective-permute-start.7 = (f32[4,1,128,128]{3,2,1,0:T(8,128)S(1)}, f32[4,1,128,128]{3,2,1,0:T(8,128)S(1)}, u32[]{:S(2)}, u32[]{:S(2)}) collective-permute-start(f32[4,1,128,128]{3,2,1,0:T(8,128)S(1)} %get-tuple-element.79), channel_id=1, source_target_pairs={{0,4},{4,8},{8,12},{1,5},{5,9},{9,13},{2,6},{6,10},{10,14},{3,7},{... | collective-permute-start | bytes 786440 | tf_op jit(solution)/shard_map/ppermute | solution.py:15
  59.1 8.1 %collective-permute-start.9 = (f32[4,1,128,128]{3,2,1,0:T(8,128)S(1)}, f32[4,1,128,128]{3,2,1,0:T(8,128)S(1)}, u32[]{:S(2)}, u32[]{:S(2)}) collective-permute-start(f32[4,1,128,128]{3,2,1,0:T(8,128)S(1)} %get-tuple-element.77), channel_id=1, source_target_pairs={{0,4},{4,8},{8,12},{1,5},{5,9},{9,13},{2,6},{6,10},{10,14},{3,7},{... | collective-permute-start | bytes 786440 | tf_op jit(solution)/shard_map/ppermute | solution.py:15
  65.8 5.4 %collective-permute-start.8 = (f32[4,1,128,128]{3,2,1,0:T(8,128)S(1)}, f32[4,1,128,128]{3,2,1,0:T(8,128)S(1)}, u32[]{:S(2)}, u32[]{:S(2)}) collective-permute-start(f32[4,1,128,128]{3,2,1,0:T(8,128)S(1)} %get-tuple-element.78), channel_id=1, source_target_pairs={{4,0},{8,4},{12,8},{5,1},{9,5},{13,9},{6,2},{10,6},{14,10},{7,3},{... | collective-permute-start | bytes 786440 | tf_op jit(solution)/shard_map/ppermute | solution.py:17
  73.2 8.4 %collective-permute-start.11 = (f32[4,1,128,128]{3,2,1,0:T(8,128)S(1)}, f32[4,1,128,128]{3,2,1,0:T(8,128)S(1)}, u32[]{:S(2)}, u32[]{:S(2)}) collective-permute-start(f32[4,1,128,128]{3,2,1,0:T(8,128)S(1)} %get-tuple-element.75), channel_id=1, source_target_pairs={{0,4},{4,8},{8,12},{1,5},{5,9},{9,13},{2,6},{6,10},{10,14},{3,7},{... | collective-permute-start | bytes 786440 | tf_op jit(solution)/shard_map/ppermute | solution.py:15
  85.6 8.0 %collective-permute-start.13 = (f32[4,1,128,128]{3,2,1,0:T(8,128)S(1)}, f32[4,1,128,128]{3,2,1,0:T(8,128)S(1)}, u32[]{:S(2)}, u32[]{:S(2)}) collective-permute-start(f32[4,1,128,128]{3,2,1,0:T(8,128)S(1)} %get-tuple-element.73), channel_id=1, source_target_pairs={{0,4},{4,8},{8,12},{1,5},{5,9},{9,13},{2,6},{6,10},{10,14},{3,7},{... | collective-permute-start | bytes 786440 | tf_op jit(solution)/shard_map/ppermute | solution.py:15
  92.1 3.4 %collective-permute-start.12 = (f32[4,1,128,128]{3,2,1,0:T(8,128)S(1)}, f32[4,1,128,128]{3,2,1,0:T(8,128)S(1)}, u32[]{:S(2)}, u32[]{:S(2)}) collective-permute-start(f32[4,1,128,128]{3,2,1,0:T(8,128)S(1)} %get-tuple-element.74), channel_id=1, source_target_pairs={{4,0},{8,4},{12,8},{5,1},{9,5},{13,9},{6,2},{10,6},{14,10},{7,3},{... | collective-permute-start | bytes 786440 | tf_op jit(solution)/shard_map/ppermute | solution.py:17
  97.5 7.7 %collective-permute-start.15 = (f32[4,1,128,128]{3,2,1,0:T(8,128)S(1)}, f32[4,1,128,128]{3,2,1,0:T(8,128)S(1)}, u32[]{:S(2)}, u32[]{:S(2)}) collective-permute-start(f32[4,1,128,128]{3,2,1,0:T(8,128)S(1)} %get-tuple-element.71), channel_id=1, source_target_pairs={{0,4},{4,8},{8,12},{1,5},{5,9},{9,13},{2,6},{6,10},{10,14},{3,7},{... | collective-permute-start | bytes 786440 | tf_op jit(solution)/shard_map/ppermute | solution.py:15
  109.2 7.9 %collective-permute-start.17 = (f32[4,1,128,128]{3,2,1,0:T(8,128)S(1)}, f32[4,1,128,128]{3,2,1,0:T(8,128)S(1)}, u32[]{:S(2)}, u32[]{:S(2)}) collective-permute-start(f32[4,1,128,128]{3,2,1,0:T(8,128)S(1)} %get-tuple-element.69), channel_id=1, source_target_pairs={{0,4},{4,8},{8,12},{1,5},{5,9},{9,13},{2,6},{6,10},{10,14},{3,7},{... | collective-permute-start | bytes 786440 | tf_op jit(solution)/shard_map/ppermute | solution.py:15
  121.1 12.7 %collective-permute-start.18 = (f32[4,2,128,128]{3,2,1,0:T(8,128)S(1)}, f32[4,2,128,128]{3,2,1,0:T(8,128)S(1)}, u32[]{:S(2)}, u32[]{:S(2)}) collective-permute-start(f32[4,2,128,128]{3,2,1,0:T(8,128)S(1)} %pad_maximum_fusion.2), channel_id=1, source_target_pairs={{0,3},{1,0},{2,1},{3,2},{4,7},{5,4},{6,5},{7,6},{8,11},{9,8},{10,9... | collective-permute-start | bytes 1572872 | tf_op jit(solution)/shard_map/ppermute | solution.py:27
  133.8 6.7 %collective-permute-start.20 = (f32[4,1,128,128]{3,2,1,0:T(8,128)S(1)}, f32[4,1,128,128]{3,2,1,0:T(8,128)S(1)}, u32[]{:S(2)}, u32[]{:S(2)}) collective-permute-start(f32[4,1,128,128]{3,2,1,0:T(8,128)S(1)} %get-tuple-element.51), channel_id=1, source_target_pairs={{0,4},{4,8},{8,12},{1,5},{5,9},{9,13},{2,6},{6,10},{10,14},{3,7},{... | collective-permute-start | bytes 786440 | tf_op jit(solution)/shard_map/ppermute | solution.py:15
  144.1 7.5 %collective-permute-start.22 = (f32[4,1,128,128]{3,2,1,0:T(8,128)S(1)}, f32[4,1,128,128]{3,2,1,0:T(8,128)S(1)}, u32[]{:S(2)}, u32[]{:S(2)}) collective-permute-start(f32[4,1,128,128]{3,2,1,0:T(8,128)S(1)} %get-tuple-element.49), channel_id=1, source_target_pairs={{0,4},{4,8},{8,12},{1,5},{5,9},{9,13},{2,6},{6,10},{10,14},{3,7},{... | collective-permute-start | bytes 786440 | tf_op jit(solution)/shard_map/ppermute | solution.py:15
  150.3 3.4 %collective-permute-start.21 = (f32[4,1,128,128]{3,2,1,0:T(8,128)S(1)}, f32[4,1,128,128]{3,2,1,0:T(8,128)S(1)}, u32[]{:S(2)}, u32[]{:S(2)}) collective-permute-start(f32[4,1,128,128]{3,2,1,0:T(8,128)S(1)} %get-tuple-element.50), channel_id=1, source_target_pairs={{4,0},{8,4},{12,8},{5,1},{9,5},{13,9},{6,2},{10,6},{14,10},{7,3},{... | collective-permute-start | bytes 786440 | tf_op jit(solution)/shard_map/ppermute | solution.py:17
  155.3 7.5 %collective-permute-start.24 = (f32[4,1,128,128]{3,2,1,0:T(8,128)S(1)}, f32[4,1,128,128]{3,2,1,0:T(8,128)S(1)}, u32[]{:S(2)}, u32[]{:S(2)}) collective-permute-start(f32[4,1,128,128]{3,2,1,0:T(8,128)S(1)} %get-tuple-element.47), channel_id=1, source_target_pairs={{0,4},{4,8},{8,12},{1,5},{5,9},{9,13},{2,6},{6,10},{10,14},{3,7},{... | collective-permute-start | bytes 786440 | tf_op jit(solution)/shard_map/ppermute | solution.py:15
  161.5 3.4 %collective-permute-start.23 = (f32[4,1,128,128]{3,2,1,0:T(8,128)S(1)}, f32[4,1,128,128]{3,2,1,0:T(8,128)S(1)}, u32[]{:S(2)}, u32[]{:S(2)}) collective-permute-start(f32[4,1,128,128]{3,2,1,0:T(8,128)S(1)} %get-tuple-element.48), channel_id=1, source_target_pairs={{4,0},{8,4},{12,8},{5,1},{9,5},{13,9},{6,2},{10,6},{14,10},{7,3},{... | collective-permute-start | bytes 786440 | tf_op jit(solution)/shard_map/ppermute | solution.py:17
  166.4 7.7 %collective-permute-start.26 = (f32[4,1,128,128]{3,2,1,0:T(8,128)S(1)}, f32[4,1,128,128]{3,2,1,0:T(8,128)S(1)}, u32[]{:S(2)}, u32[]{:S(2)}) collective-permute-start(f32[4,1,128,128]{3,2,1,0:T(8,128)S(1)} %get-tuple-element.45), channel_id=1, source_target_pairs={{0,4},{4,8},{8,12},{1,5},{5,9},{9,13},{2,6},{6,10},{10,14},{3,7},{... | collective-permute-start | bytes 786440 | tf_op jit(solution)/shard_map/ppermute | solution.py:15
  172.6 3.4 %collective-permute-start.25 = (f32[4,1,128,128]{3,2,1,0:T(8,128)S(1)}, f32[4,1,128,128]{3,2,1,0:T(8,128)S(1)}, u32[]{:S(2)}, u32[]{:S(2)}) collective-permute-start(f32[4,1,128,128]{3,2,1,0:T(8,128)S(1)} %get-tuple-element.46), channel_id=1, source_target_pairs={{4,0},{8,4},{12,8},{5,1},{9,5},{13,9},{6,2},{10,6},{14,10},{7,3},{... | collective-permute-start | bytes 786440 | tf_op jit(solution)/shard_map/ppermute | solution.py:17
  177.6 7.5 %collective-permute-start.28 = (f32[4,1,128,128]{3,2,1,0:T(8,128)S(1)}, f32[4,1,128,128]{3,2,1,0:T(8,128)S(1)}, u32[]{:S(2)}, u32[]{:S(2)}) collective-permute-start(f32[4,1,128,128]{3,2,1,0:T(8,128)S(1)} %get-tuple-element.43), channel_id=1, source_target_pairs={{0,4},{4,8},{8,12},{1,5},{5,9},{9,13},{2,6},{6,10},{10,14},{3,7},{... | collective-permute-start | bytes 786440 | tf_op jit(solution)/shard_map/ppermute | solution.py:15
  183.8 3.4 %collective-permute-start.27 = (f32[4,1,128,128]{3,2,1,0:T(8,128)S(1)}, f32[4,1,128,128]{3,2,1,0:T(8,128)S(1)}, u32[]{:S(2)}, u32[]{:S(2)}) collective-permute-start(f32[4,1,128,128]{3,2,1,0:T(8,128)S(1)} %get-tuple-element.44), channel_id=1, source_target_pairs={{4,0},{8,4},{12,8},{5,1},{9,5},{13,9},{6,2},{10,6},{14,10},{7,3},{... | collective-permute-start | bytes 786440 | tf_op jit(solution)/shard_map/ppermute | solution.py:17
  188.7 7.5 %collective-permute-start.30 = (f32[4,1,128,128]{3,2,1,0:T(8,128)S(1)}, f32[4,1,128,128]{3,2,1,0:T(8,128)S(1)}, u32[]{:S(2)}, u32[]{:S(2)}) collective-permute-start(f32[4,1,128,128]{3,2,1,0:T(8,128)S(1)} %get-tuple-element.41), channel_id=1, source_target_pairs={{0,4},{4,8},{8,12},{1,5},{5,9},{9,13},{2,6},{6,10},{10,14},{3,7},{... | collective-permute-start | bytes 786440 | tf_op jit(solution)/shard_map/ppermute | solution.py:15
  194.9 3.4 %collective-permute-start.29 = (f32[4,1,128,128]{3,2,1,0:T(8,128)S(1)}, f32[4,1,128,128]{3,2,1,0:T(8,128)S(1)}, u32[]{:S(2)}, u32[]{:S(2)}) collective-permute-start(f32[4,1,128,128]{3,2,1,0:T(8,128)S(1)} %get-tuple-element.42), channel_id=1, source_target_pairs={{4,0},{8,4},{12,8},{5,1},{9,5},{13,9},{6,2},{10,6},{14,10},{7,3},{... | collective-permute-start | bytes 786440 | tf_op jit(solution)/shard_map/ppermute | solution.py:17
  199.8 7.5 %collective-permute-start.32 = (f32[4,1,128,128]{3,2,1,0:T(8,128)S(1)}, f32[4,1,128,128]{3,2,1,0:T(8,128)S(1)}, u32[]{:S(2)}, u32[]{:S(2)}) collective-permute-start(f32[4,1,128,128]{3,2,1,0:T(8,128)S(1)} %get-tuple-element.39), channel_id=1, source_target_pairs={{0,4},{4,8},{8,12},{1,5},{5,9},{9,13},{2,6},{6,10},{10,14},{3,7},{... | collective-permute-start | bytes 786440 | tf_op jit(solution)/shard_map/ppermute | solution.py:15
  206.0 3.4 %collective-permute-start.31 = (f32[4,1,128,128]{3,2,1,0:T(8,128)S(1)}, f32[4,1,128,128]{3,2,1,0:T(8,128)S(1)}, u32[]{:S(2)}, u32[]{:S(2)}) collective-permute-start(f32[4,1,128,128]{3,2,1,0:T(8,128)S(1)} %get-tuple-element.40), channel_id=1, source_target_pairs={{4,0},{8,4},{12,8},{5,1},{9,5},{13,9},{6,2},{10,6},{14,10},{7,3},{... | collective-permute-start | bytes 786440 | tf_op jit(solution)/shard_map/ppermute | solution.py:17
  213.1 43.1 %collective-permute-start.34 = (f32[4,1,128,128]{3,2,1,0:T(8,128)S(1)}, f32[4,1,128,128]{3,2,1,0:T(8,128)S(1)}, u32[]{:S(2)}, u32[]{:S(2)}) collective-permute-start(f32[4,1,128,128]{3,2,1,0:T(8,128)S(1)} %get-tuple-element.37), channel_id=1, source_target_pairs={{0,4},{4,8},{8,12},{1,5},{5,9},{9,13},{2,6},{6,10},{10,14},{3,7},{... | collective-permute-start | bytes 786440 | tf_op jit(solution)/shard_map/ppermute | solution.py:15
  219.3 36.9 %collective-permute-start.33 = (f32[4,1,128,128]{3,2,1,0:T(8,128)S(1)}, f32[4,1,128,128]{3,2,1,0:T(8,128)S(1)}, u32[]{:S(2)}, u32[]{:S(2)}) collective-permute-start(f32[4,1,128,128]{3,2,1,0:T(8,128)S(1)} %get-tuple-element.38), channel_id=1, source_target_pairs={{4,0},{8,4},{12,8},{5,1},{9,5},{13,9},{6,2},{10,6},{14,10},{7,3},{... | collective-permute-start | bytes 786440 | tf_op jit(solution)/shard_map/ppermute | solution.py:17
  (63 other events, 145.3 us)
Sparse Core Ops, SparseCore 0:
  219.4 35.3 all-reduce.21
where the time goes:
time: 267 us; the launch traced here: 266 us
  starting transfers between devices  125 us (47%)
  waiting for transfers between devices  71 us (27%)
  other arithmetic  37.5 us (14%)
  local copies, waits for them, and re-layouts  16.4 us (6%)
  between operations  16.1 us (6%)
    ppermute x17, starting transfers between devices, padded(): lax.ppermute(tail, axis, [(i, (i + 1) % count) for i in range(ends)])  99 us
    psum x1, waiting for transfers between devices, body(): summed = lax.psum(partial_sum, 'arc')  34.2 us
    ppermute x17, waiting for transfers between devices, padded(): lax.ppermute(head, axis, [((i + 1) % count, i) for i in range(ends)])  26 us
    ppermute x17, starting transfers between devices, padded(): lax.ppermute(head, axis, [((i + 1) % count, i) for i in range(ends)])  22.3 us
    ppermute x1, waiting for transfers between devices, passed_along(): return lax.ppermute(value, axis, pairs)  9.02 us
    concatenate x16, other arithmetic, padded(): jnp.concatenate([lax.ppermute(tail, axis, [(i, (i + 1) % count) for i in...  8.71 us
    unnamed x120, local copies, waits for them, and re-layouts  8.05 us
    add x14, other arithmetic, adjoint_update(): a_now + 0.1 * (1.2 * laplace(ext_a) + carry_a - alpha * a_now - current_a...  7.44 us
  transfers between devices with their start and end apart: 36, of which 16 were waited for; matrix products, arithmetic and copies ran while one was open for 7% of the time, Pallas kernels for 0%

commit v1 on v0

--- a/solution.py
+++ b/solution.py
@@ -159,7 +159,7 @@
     for interior_block in range(device_instant_total - 1, -1, -1):
         adj, summand_contribution = one_step(adj, interior_block)
         partial_sum = partial_sum + summand_contribution
-    summed = lax.psum(partial_sum, "arc")
+    summed = jnp.sum(lax.all_gather(partial_sum, "arc"), axis=0)
     share = summed.shape[1] // lax.axis_size("arc")
     gradient = lax.dynamic_slice_in_dim(summed, lax.axis_index("arc") * share, share, 1)
     return (gradient, adj[None])

time: 267 us -> 242 us (0.906)
  waiting for transfers between devices: 71 us -> 36.2 us
  blocking collectives: 0 us -> 16.9 us
  between operations: 16.1 us -> 2.85 us
  other arithmetic: 37.5 us -> 42 us
    psum x1 -> x0, waiting for transfers between devices: 34.2 us -> none  [body(): summed = lax.psum(partial_sum, 'arc')]
    all_gather x0 -> x1, blocking collectives: none -> 16.9 us  [body(): summed = jnp.sum(lax.all_gather(partial_sum, 'arc'), axis=0)]
    unnamed x120 -> x162, local copies, waits for them, and re-layouts: 8.05 us -> 9.56 us
  transfers between devices with their start and end apart: 36 -> 35, of which waited for: 16 -> 15; matrix products, arithmetic and copies ran while one was open for 7% -> 7% of each run, Pallas kernels for 0% -> 0%
where the time goes in v1:
time: 242 us; the launch traced here: 241 us
  starting transfers between devices  126 us (52%)
  other arithmetic  42 us (17%)
  waiting for transfers between devices  36.2 us (15%)
  local copies, waits for them, and re-layouts  17.1 us (7%)
  blocking collectives  16.9 us (7%)
  between operations  2.85 us (1%)
    ppermute x17, starting transfers between devices, padded(): lax.ppermute(tail, axis, [(i, (i + 1) % count) for i in range(ends)])  99.5 us
    ppermute x17, waiting for transfers between devices, padded(): lax.ppermute(head, axis, [((i + 1) % count, i) for i in range(ends)])  25.4 us
    ppermute x17, starting transfers between devices, padded(): lax.ppermute(head, axis, [((i + 1) % count, i) for i in range(ends)])  22.5 us
    all_gather x1, blocking collectives, body(): summed = jnp.sum(lax.all_gather(partial_sum, 'arc'), axis=0)  16.9 us
    concatenate x16, other arithmetic, padded(): jnp.concatenate([lax.ppermute(tail, axis, [(i, (i + 1) % count) for i in...  9.86 us
    unnamed x162, local copies, waits for them, and re-layouts  9.56 us
    ppermute x1, waiting for transfers between devices, passed_along(): return lax.ppermute(value, axis, pairs)  9.02 us
    add x14, other arithmetic, adjoint_update(): a_now + 0.1 * (1.2 * laplace(ext_a) + carry_a - alpha * a_now - current_a...  7.47 us
  transfers between devices with their start and end apart: 35, of which 15 were waited for; matrix products, arithmetic and copies ran while one was open for 7% of the time, Pallas kernels for 0%

profile of v1, /device:TPU:0, one launch (start us, length us, event | category | flops | bytes accessed | tf_op | source)
XLA Modules:
  0.0 240.7 jit_solution(7011193559931998268)
XLA Ops:
  2.8 3.7 %collective-permute-start.1 = (f32[4,1,128,128]{3,2,1,0:T(8,128)}, f32[4,1,128,128]{3,2,1,0:T(8,128)}, u32[]{:S(2)}, u32[]{:S(2)}) collective-permute-start(f32[4,1,128,128]{3,2,1,0:T(8,128)} %broadcast.302), channel_id=1, source_target_pairs={{0,4},{4,8},{8,12},{1,5},{5,9},{9,13},{2,6},{6,10},{10,14},{3,7},{... | collective-permute-start | bytes 786440 | tf_op jit(solution)/shard_map/ppermute | solution.py:15
  8.4 4.5 %collective-permute-start.2 = (bf16[8,1,128,128]{3,2,1,0:T(8,128)(2,1)}, bf16[8,1,128,128]{3,2,1,0:T(8,128)(2,1)}, u32[]{:S(2)}, u32[]{:S(2)}) collective-permute-start(bf16[8,1,128,128]{3,2,1,0:T(8,128)(2,1)} %get-tuple-element.84), channel_id=1, source_target_pairs={{0,4},{4,8},{8,12},{1,5},{5,9},{9,13},{2,6},{6,10},{10,14},{3,7},{... | collective-permute-start | bytes 786440 | tf_op jit(solution)/shard_map/ppermute | solution.py:15
  35.1 3.7 %collective-permute-start.5 = (f32[4,1,128,128]{3,2,1,0:T(8,128)S(1)}, f32[4,1,128,128]{3,2,1,0:T(8,128)S(1)}, u32[]{:S(2)}, u32[]{:S(2)}) collective-permute-start(f32[4,1,128,128]{3,2,1,0:T(8,128)S(1)} %get-tuple-element.81), channel_id=1, source_target_pairs={{0,4},{4,8},{8,12},{1,5},{5,9},{9,13},{2,6},{6,10},{10,14},{3,7},{... | collective-permute-start | bytes 786440 | tf_op jit(solution)/shard_map/ppermute | solution.py:15
  43.5 6.4 %collective-permute-start.7 = (f32[4,1,128,128]{3,2,1,0:T(8,128)S(1)}, f32[4,1,128,128]{3,2,1,0:T(8,128)S(1)}, u32[]{:S(2)}, u32[]{:S(2)}) collective-permute-start(f32[4,1,128,128]{3,2,1,0:T(8,128)S(1)} %get-tuple-element.79), channel_id=1, source_target_pairs={{0,4},{4,8},{8,12},{1,5},{5,9},{9,13},{2,6},{6,10},{10,14},{3,7},{... | collective-permute-start | bytes 786440 | tf_op jit(solution)/shard_map/ppermute | solution.py:15
  53.1 6.6 %collective-permute-start.9 = (f32[4,1,128,128]{3,2,1,0:T(8,128)S(1)}, f32[4,1,128,128]{3,2,1,0:T(8,128)S(1)}, u32[]{:S(2)}, u32[]{:S(2)}) collective-permute-start(f32[4,1,128,128]{3,2,1,0:T(8,128)S(1)} %get-tuple-element.77), channel_id=1, source_target_pairs={{0,4},{4,8},{8,12},{1,5},{5,9},{9,13},{2,6},{6,10},{10,14},{3,7},{... | collective-permute-start | bytes 786440 | tf_op jit(solution)/shard_map/ppermute | solution.py:15
  61.2 3.9 %collective-permute-done.8 = f32[4,1,128,128]{3,2,1,0:T(8,128)S(1)} collective-permute-done((f32[4,1,128,128]{3,2,1,0:T(8,128)S(1)}, f32[4,1,128,128]{3,2,1,0:T(8,128)S(1)}, u32[]{:S(2)}, u32[]{:S(2)}) %collective-permute-start.8) | collective-permute-done | bytes 262176 | tf_op jit(solution)/shard_map/ppermute | solution.py:17
  67.2 6.7 %collective-permute-start.11 = (f32[4,1,128,128]{3,2,1,0:T(8,128)S(1)}, f32[4,1,128,128]{3,2,1,0:T(8,128)S(1)}, u32[]{:S(2)}, u32[]{:S(2)}) collective-permute-start(f32[4,1,128,128]{3,2,1,0:T(8,128)S(1)} %get-tuple-element.75), channel_id=1, source_target_pairs={{0,4},{4,8},{8,12},{1,5},{5,9},{9,13},{2,6},{6,10},{10,14},{3,7},{... | collective-permute-start | bytes 786440 | tf_op jit(solution)/shard_map/ppermute | solution.py:15
  75.6 1.9 collective-permute-done.10
  79.5 6.2 %collective-permute-start.13 = (f32[4,1,128,128]{3,2,1,0:T(8,128)S(1)}, f32[4,1,128,128]{3,2,1,0:T(8,128)S(1)}, u32[]{:S(2)}, u32[]{:S(2)}) collective-permute-start(f32[4,1,128,128]{3,2,1,0:T(8,128)S(1)} %get-tuple-element.73), channel_id=1, source_target_pairs={{0,4},{4,8},{8,12},{1,5},{5,9},{9,13},{2,6},{6,10},{10,14},{3,7},{... | collective-permute-start | bytes 786440 | tf_op jit(solution)/shard_map/ppermute | solution.py:15
  87.5 1.9 collective-permute-done.12
  91.5 6.2 %collective-permute-start.15 = (f32[4,1,128,128]{3,2,1,0:T(8,128)S(1)}, f32[4,1,128,128]{3,2,1,0:T(8,128)S(1)}, u32[]{:S(2)}, u32[]{:S(2)}) collective-permute-start(f32[4,1,128,128]{3,2,1,0:T(8,128)S(1)} %get-tuple-element.71), channel_id=1, source_target_pairs={{0,4},{4,8},{8,12},{1,5},{5,9},{9,13},{2,6},{6,10},{10,14},{3,7},{... | collective-permute-start | bytes 786440 | tf_op jit(solution)/shard_map/ppermute | solution.py:15
  99.3 1.9 collective-permute-done.14
  103.3 6.2 %collective-permute-start.17 = (f32[4,1,128,128]{3,2,1,0:T(8,128)S(1)}, f32[4,1,128,128]{3,2,1,0:T(8,128)S(1)}, u32[]{:S(2)}, u32[]{:S(2)}) collective-permute-start(f32[4,1,128,128]{3,2,1,0:T(8,128)S(1)} %get-tuple-element.69), channel_id=1, source_target_pairs={{0,4},{4,8},{8,12},{1,5},{5,9},{9,13},{2,6},{6,10},{10,14},{3,7},{... | collective-permute-start | bytes 786440 | tf_op jit(solution)/shard_map/ppermute | solution.py:15
  111.2 1.9 collective-permute-done.16
  115.1 3.7 %collective-permute-start.18 = (f32[4,2,128,128]{3,2,1,0:T(8,128)S(1)}, f32[4,2,128,128]{3,2,1,0:T(8,128)S(1)}, u32[]{:S(2)}, u32[]{:S(2)}) collective-permute-start(f32[4,2,128,128]{3,2,1,0:T(8,128)S(1)} %pad_maximum_fusion.2), channel_id=1, source_target_pairs={{0,3},{1,0},{2,1},{3,2},{4,7},{5,4},{6,5},{7,6},{8,11},{9,8},{10,9... | collective-permute-start | bytes 1572872 | tf_op jit(solution)/shard_map/ppermute | solution.py:27
  118.8 9.0 %collective-permute-done.18 = f32[4,2,128,128]{3,2,1,0:T(8,128)S(1)} collective-permute-done((f32[4,2,128,128]{3,2,1,0:T(8,128)S(1)}, f32[4,2,128,128]{3,2,1,0:T(8,128)S(1)}, u32[]{:S(2)}, u32[]{:S(2)}) %collective-permute-start.18) | collective-permute-done | bytes 524320 | tf_op jit(solution)/shard_map/ppermute | solution.py:27
  127.9 5.3 %collective-permute-start.20 = (f32[4,1,128,128]{3,2,1,0:T(8,128)S(1)}, f32[4,1,128,128]{3,2,1,0:T(8,128)S(1)}, u32[]{:S(2)}, u32[]{:S(2)}) collective-permute-start(f32[4,1,128,128]{3,2,1,0:T(8,128)S(1)} %get-tuple-element.51), channel_id=1, source_target_pairs={{0,4},{4,8},{8,12},{1,5},{5,9},{9,13},{2,6},{6,10},{10,14},{3,7},{... | collective-permute-start | bytes 786440 | tf_op jit(solution)/shard_map/ppermute | solution.py:15
  134.6 2.1 collective-permute-done.19
  138.2 6.2 %collective-permute-start.22 = (f32[4,1,128,128]{3,2,1,0:T(8,128)S(1)}, f32[4,1,128,128]{3,2,1,0:T(8,128)S(1)}, u32[]{:S(2)}, u32[]{:S(2)}) collective-permute-start(f32[4,1,128,128]{3,2,1,0:T(8,128)S(1)} %get-tuple-element.49), channel_id=1, source_target_pairs={{0,4},{4,8},{8,12},{1,5},{5,9},{9,13},{2,6},{6,10},{10,14},{3,7},{... | collective-permute-start | bytes 786440 | tf_op jit(solution)/shard_map/ppermute | solution.py:15
  145.7 2.1 collective-permute-done.21
  149.3 6.2 %collective-permute-start.24 = (f32[4,1,128,128]{3,2,1,0:T(8,128)S(1)}, f32[4,1,128,128]{3,2,1,0:T(8,128)S(1)}, u32[]{:S(2)}, u32[]{:S(2)}) collective-permute-start(f32[4,1,128,128]{3,2,1,0:T(8,128)S(1)} %get-tuple-element.47), channel_id=1, source_target_pairs={{0,4},{4,8},{8,12},{1,5},{5,9},{9,13},{2,6},{6,10},{10,14},{3,7},{... | collective-permute-start | bytes 786440 | tf_op jit(solution)/shard_map/ppermute | solution.py:15
  156.8 2.1 collective-permute-done.23
  160.5 6.2 %collective-permute-start.26 = (f32[4,1,128,128]{3,2,1,0:T(8,128)S(1)}, f32[4,1,128,128]{3,2,1,0:T(8,128)S(1)}, u32[]{:S(2)}, u32[]{:S(2)}) collective-permute-start(f32[4,1,128,128]{3,2,1,0:T(8,128)S(1)} %get-tuple-element.45), channel_id=1, source_target_pairs={{0,4},{4,8},{8,12},{1,5},{5,9},{9,13},{2,6},{6,10},{10,14},{3,7},{... | collective-permute-start | bytes 786440 | tf_op jit(solution)/shard_map/ppermute | solution.py:15
  168.2 1.9 collective-permute-done.25
  171.6 6.2 %collective-permute-start.28 = (f32[4,1,128,128]{3,2,1,0:T(8,128)S(1)}, f32[4,1,128,128]{3,2,1,0:T(8,128)S(1)}, u32[]{:S(2)}, u32[]{:S(2)}) collective-permute-start(f32[4,1,128,128]{3,2,1,0:T(8,128)S(1)} %get-tuple-element.43), channel_id=1, source_target_pairs={{0,4},{4,8},{8,12},{1,5},{5,9},{9,13},{2,6},{6,10},{10,14},{3,7},{... | collective-permute-start | bytes 786440 | tf_op jit(solution)/shard_map/ppermute | solution.py:15
  179.1 2.1 collective-permute-done.27
  182.8 6.3 %collective-permute-start.30 = (f32[4,1,128,128]{3,2,1,0:T(8,128)S(1)}, f32[4,1,128,128]{3,2,1,0:T(8,128)S(1)}, u32[]{:S(2)}, u32[]{:S(2)}) collective-permute-start(f32[4,1,128,128]{3,2,1,0:T(8,128)S(1)} %get-tuple-element.41), channel_id=1, source_target_pairs={{0,4},{4,8},{8,12},{1,5},{5,9},{9,13},{2,6},{6,10},{10,14},{3,7},{... | collective-permute-start | bytes 786440 | tf_op jit(solution)/shard_map/ppermute | solution.py:15
  190.4 2.1 collective-permute-done.29
  195.6 6.9 %collective-permute-start.32 = (f32[4,1,128,128]{3,2,1,0:T(8,128)}, f32[4,1,128,128]{3,2,1,0:T(8,128)}, u32[]{:S(2)}, u32[]{:S(2)}) collective-permute-start(f32[4,1,128,128]{3,2,1,0:T(8,128)} %get-tuple-element.39), channel_id=1, source_target_pairs={{0,4},{4,8},{8,12},{1,5},{5,9},{9,13},{2,6},{6,10},{10,14},{3,7},{... | collective-permute-start | bytes 786440 | tf_op jit(solution)/shard_map/ppermute | solution.py:15
  209.1 2.2 fusion.10
  213.4 6.1 %collective-permute-start.34 = (f32[4,1,128,128]{3,2,1,0:T(8,128)S(1)}, f32[4,1,128,128]{3,2,1,0:T(8,128)S(1)}, u32[]{:S(2)}, u32[]{:S(2)}) collective-permute-start(f32[4,1,128,128]{3,2,1,0:T(8,128)S(1)} %get-tuple-element.37), channel_id=1, source_target_pairs={{0,4},{4,8},{8,12},{1,5},{5,9},{9,13},{2,6},{6,10},{10,14},{3,7},{... | collective-permute-start | bytes 786440 | tf_op jit(solution)/shard_map/ppermute | solution.py:15
  219.5 16.9 %all-gather = f32[8,128,128]{2,1,0:T(8,128)S(1)} all-gather(f32[2,128,128]{2,1,0:T(8,128)S(1)} %get-tuple-element.10), channel_id=2, replica_groups=mesh['job'=2,'space'=4,'arc'=4] {'arc'}, dimensions={0}, use_global_device_ids=true | all-gather | bytes 655360 | tf_op jit(solution)/shard_map/all_gather | solution.py:162
  (412 shorter events, 82.7 us)
Async XLA Ops:
  1.4 28.3 %collective-permute-start = (f32[4,1,128,128]{3,2,1,0:T(8,128)}, f32[4,1,128,128]{3,2,1,0:T(8,128)}, u32[]{:S(2)}, u32[]{:S(2)}) collective-permute-start(f32[4,1,128,128]{3,2,1,0:T(8,128)} %broadcast.302), channel_id=1, source_target_pairs={{4,0},{8,4},{12,8},{5,1},{9,5},{13,9},{6,2},{10,6},{14,10},{7,3},{... | collective-permute-start | bytes 786440 | tf_op jit(solution)/shard_map/ppermute | solution.py:17
  2.8 25.8 %collective-permute-start.1 = (f32[4,1,128,128]{3,2,1,0:T(8,128)}, f32[4,1,128,128]{3,2,1,0:T(8,128)}, u32[]{:S(2)}, u32[]{:S(2)}) collective-permute-start(f32[4,1,128,128]{3,2,1,0:T(8,128)} %broadcast.302), channel_id=1, source_target_pairs={{0,4},{4,8},{8,12},{1,5},{5,9},{9,13},{2,6},{6,10},{10,14},{3,7},{... | collective-permute-start | bytes 786440 | tf_op jit(solution)/shard_map/ppermute | solution.py:15
  8.4 14.1 %collective-permute-start.2 = (bf16[8,1,128,128]{3,2,1,0:T(8,128)(2,1)}, bf16[8,1,128,128]{3,2,1,0:T(8,128)(2,1)}, u32[]{:S(2)}, u32[]{:S(2)}) collective-permute-start(bf16[8,1,128,128]{3,2,1,0:T(8,128)(2,1)} %get-tuple-element.84), channel_id=1, source_target_pairs={{0,4},{4,8},{8,12},{1,5},{5,9},{9,13},{2,6},{6,10},{10,14},{3,7},{... | collective-permute-start | bytes 786440 | tf_op jit(solution)/shard_map/ppermute | solution.py:15
  12.9 10.6 %collective-permute-start.3 = (bf16[8,1,128,128]{3,2,1,0:T(8,128)(2,1)}, bf16[8,1,128,128]{3,2,1,0:T(8,128)(2,1)}, u32[]{:S(2)}, u32[]{:S(2)}) collective-permute-start(bf16[8,1,128,128]{3,2,1,0:T(8,128)(2,1)} %get-tuple-element.83), channel_id=1, source_target_pairs={{4,0},{8,4},{12,8},{5,1},{9,5},{13,9},{6,2},{10,6},{14,10},{7,3},{... | collective-permute-start | bytes 786440 | tf_op jit(solution)/shard_map/ppermute | solution.py:17
  33.8 5.2 %collective-permute-start.4 = (f32[4,1,128,128]{3,2,1,0:T(8,128)S(1)}, f32[4,1,128,128]{3,2,1,0:T(8,128)S(1)}, u32[]{:S(2)}, u32[]{:S(2)}) collective-permute-start(f32[4,1,128,128]{3,2,1,0:T(8,128)S(1)} %get-tuple-element.82), channel_id=1, source_target_pairs={{4,0},{8,4},{12,8},{5,1},{9,5},{13,9},{6,2},{10,6},{14,10},{7,3},{... | collective-permute-start | bytes 786440 | tf_op jit(solution)/shard_map/ppermute | solution.py:17
  35.1 4.8 %collective-permute-start.5 = (f32[4,1,128,128]{3,2,1,0:T(8,128)S(1)}, f32[4,1,128,128]{3,2,1,0:T(8,128)S(1)}, u32[]{:S(2)}, u32[]{:S(2)}) collective-permute-start(f32[4,1,128,128]{3,2,1,0:T(8,128)S(1)} %get-tuple-element.81), channel_id=1, source_target_pairs={{0,4},{4,8},{8,12},{1,5},{5,9},{9,13},{2,6},{6,10},{10,14},{3,7},{... | collective-permute-start | bytes 786440 | tf_op jit(solution)/shard_map/ppermute | solution.py:15
  42.1 8.0 %collective-permute-start.6 = (f32[4,1,128,128]{3,2,1,0:T(8,128)S(1)}, f32[4,1,128,128]{3,2,1,0:T(8,128)S(1)}, u32[]{:S(2)}, u32[]{:S(2)}) collective-permute-start(f32[4,1,128,128]{3,2,1,0:T(8,128)S(1)} %get-tuple-element.80), channel_id=1, source_target_pairs={{4,0},{8,4},{12,8},{5,1},{9,5},{13,9},{6,2},{10,6},{14,10},{7,3},{... | collective-permute-start | bytes 786440 | tf_op jit(solution)/shard_map/ppermute | solution.py:17
  43.5 7.6 %collective-permute-start.7 = (f32[4,1,128,128]{3,2,1,0:T(8,128)S(1)}, f32[4,1,128,128]{3,2,1,0:T(8,128)S(1)}, u32[]{:S(2)}, u32[]{:S(2)}) collective-permute-start(f32[4,1,128,128]{3,2,1,0:T(8,128)S(1)} %get-tuple-element.79), channel_id=1, source_target_pairs={{0,4},{4,8},{8,12},{1,5},{5,9},{9,13},{2,6},{6,10},{10,14},{3,7},{... | collective-permute-start | bytes 786440 | tf_op jit(solution)/shard_map/ppermute | solution.py:15
  53.1 8.1 %collective-permute-start.9 = (f32[4,1,128,128]{3,2,1,0:T(8,128)S(1)}, f32[4,1,128,128]{3,2,1,0:T(8,128)S(1)}, u32[]{:S(2)}, u32[]{:S(2)}) collective-permute-start(f32[4,1,128,128]{3,2,1,0:T(8,128)S(1)} %get-tuple-element.77), channel_id=1, source_target_pairs={{0,4},{4,8},{8,12},{1,5},{5,9},{9,13},{2,6},{6,10},{10,14},{3,7},{... | collective-permute-start | bytes 786440 | tf_op jit(solution)/shard_map/ppermute | solution.py:15
  59.7 5.4 %collective-permute-start.8 = (f32[4,1,128,128]{3,2,1,0:T(8,128)S(1)}, f32[4,1,128,128]{3,2,1,0:T(8,128)S(1)}, u32[]{:S(2)}, u32[]{:S(2)}) collective-permute-start(f32[4,1,128,128]{3,2,1,0:T(8,128)S(1)} %get-tuple-element.78), channel_id=1, source_target_pairs={{4,0},{8,4},{12,8},{5,1},{9,5},{13,9},{6,2},{10,6},{14,10},{7,3},{... | collective-permute-start | bytes 786440 | tf_op jit(solution)/shard_map/ppermute | solution.py:17
  67.2 8.4 %collective-permute-start.11 = (f32[4,1,128,128]{3,2,1,0:T(8,128)S(1)}, f32[4,1,128,128]{3,2,1,0:T(8,128)S(1)}, u32[]{:S(2)}, u32[]{:S(2)}) collective-permute-start(f32[4,1,128,128]{3,2,1,0:T(8,128)S(1)} %get-tuple-element.75), channel_id=1, source_target_pairs={{0,4},{4,8},{8,12},{1,5},{5,9},{9,13},{2,6},{6,10},{10,14},{3,7},{... | collective-permute-start | bytes 786440 | tf_op jit(solution)/shard_map/ppermute | solution.py:15
  74.1 3.4 %collective-permute-start.10 = (f32[4,1,128,128]{3,2,1,0:T(8,128)S(1)}, f32[4,1,128,128]{3,2,1,0:T(8,128)S(1)}, u32[]{:S(2)}, u32[]{:S(2)}) collective-permute-start(f32[4,1,128,128]{3,2,1,0:T(8,128)S(1)} %get-tuple-element.76), channel_id=1, source_target_pairs={{4,0},{8,4},{12,8},{5,1},{9,5},{13,9},{6,2},{10,6},{14,10},{7,3},{... | collective-permute-start | bytes 786440 | tf_op jit(solution)/shard_map/ppermute | solution.py:17
  79.5 8.0 %collective-permute-start.13 = (f32[4,1,128,128]{3,2,1,0:T(8,128)S(1)}, f32[4,1,128,128]{3,2,1,0:T(8,128)S(1)}, u32[]{:S(2)}, u32[]{:S(2)}) collective-permute-start(f32[4,1,128,128]{3,2,1,0:T(8,128)S(1)} %get-tuple-element.73), channel_id=1, source_target_pairs={{0,4},{4,8},{8,12},{1,5},{5,9},{9,13},{2,6},{6,10},{10,14},{3,7},{... | collective-permute-start | bytes 786440 | tf_op jit(solution)/shard_map/ppermute | solution.py:15
  85.9 3.6 %collective-permute-start.12 = (f32[4,1,128,128]{3,2,1,0:T(8,128)S(1)}, f32[4,1,128,128]{3,2,1,0:T(8,128)S(1)}, u32[]{:S(2)}, u32[]{:S(2)}) collective-permute-start(f32[4,1,128,128]{3,2,1,0:T(8,128)S(1)} %get-tuple-element.74), channel_id=1, source_target_pairs={{4,0},{8,4},{12,8},{5,1},{9,5},{13,9},{6,2},{10,6},{14,10},{7,3},{... | collective-permute-start | bytes 786440 | tf_op jit(solution)/shard_map/ppermute | solution.py:17
  91.5 7.7 %collective-permute-start.15 = (f32[4,1,128,128]{3,2,1,0:T(8,128)S(1)}, f32[4,1,128,128]{3,2,1,0:T(8,128)S(1)}, u32[]{:S(2)}, u32[]{:S(2)}) collective-permute-start(f32[4,1,128,128]{3,2,1,0:T(8,128)S(1)} %get-tuple-element.71), channel_id=1, source_target_pairs={{0,4},{4,8},{8,12},{1,5},{5,9},{9,13},{2,6},{6,10},{10,14},{3,7},{... | collective-permute-start | bytes 786440 | tf_op jit(solution)/shard_map/ppermute | solution.py:15
  97.8 3.4 %collective-permute-start.14 = (f32[4,1,128,128]{3,2,1,0:T(8,128)S(1)}, f32[4,1,128,128]{3,2,1,0:T(8,128)S(1)}, u32[]{:S(2)}, u32[]{:S(2)}) collective-permute-start(f32[4,1,128,128]{3,2,1,0:T(8,128)S(1)} %get-tuple-element.72), channel_id=1, source_target_pairs={{4,0},{8,4},{12,8},{5,1},{9,5},{13,9},{6,2},{10,6},{14,10},{7,3},{... | collective-permute-start | bytes 786440 | tf_op jit(solution)/shard_map/ppermute | solution.py:17
  103.3 7.9 %collective-permute-start.17 = (f32[4,1,128,128]{3,2,1,0:T(8,128)S(1)}, f32[4,1,128,128]{3,2,1,0:T(8,128)S(1)}, u32[]{:S(2)}, u32[]{:S(2)}) collective-permute-start(f32[4,1,128,128]{3,2,1,0:T(8,128)S(1)} %get-tuple-element.69), channel_id=1, source_target_pairs={{0,4},{4,8},{8,12},{1,5},{5,9},{9,13},{2,6},{6,10},{10,14},{3,7},{... | collective-permute-start | bytes 786440 | tf_op jit(solution)/shard_map/ppermute | solution.py:15
  109.7 3.4 %collective-permute-start.16 = (f32[4,1,128,128]{3,2,1,0:T(8,128)S(1)}, f32[4,1,128,128]{3,2,1,0:T(8,128)S(1)}, u32[]{:S(2)}, u32[]{:S(2)}) collective-permute-start(f32[4,1,128,128]{3,2,1,0:T(8,128)S(1)} %get-tuple-element.70), channel_id=1, source_target_pairs={{4,0},{8,4},{12,8},{5,1},{9,5},{13,9},{6,2},{10,6},{14,10},{7,3},{... | collective-permute-start | bytes 786440 | tf_op jit(solution)/shard_map/ppermute | solution.py:17
  115.1 12.7 %collective-permute-start.18 = (f32[4,2,128,128]{3,2,1,0:T(8,128)S(1)}, f32[4,2,128,128]{3,2,1,0:T(8,128)S(1)}, u32[]{:S(2)}, u32[]{:S(2)}) collective-permute-start(f32[4,2,128,128]{3,2,1,0:T(8,128)S(1)} %pad_maximum_fusion.2), channel_id=1, source_target_pairs={{0,3},{1,0},{2,1},{3,2},{4,7},{5,4},{6,5},{7,6},{8,11},{9,8},{10,9... | collective-permute-start | bytes 1572872 | tf_op jit(solution)/shard_map/ppermute | solution.py:27
  127.9 6.7 %collective-permute-start.20 = (f32[4,1,128,128]{3,2,1,0:T(8,128)S(1)}, f32[4,1,128,128]{3,2,1,0:T(8,128)S(1)}, u32[]{:S(2)}, u32[]{:S(2)}) collective-permute-start(f32[4,1,128,128]{3,2,1,0:T(8,128)S(1)} %get-tuple-element.51), channel_id=1, source_target_pairs={{0,4},{4,8},{8,12},{1,5},{5,9},{9,13},{2,6},{6,10},{10,14},{3,7},{... | collective-permute-start | bytes 786440 | tf_op jit(solution)/shard_map/ppermute | solution.py:15
  138.2 7.5 %collective-permute-start.22 = (f32[4,1,128,128]{3,2,1,0:T(8,128)S(1)}, f32[4,1,128,128]{3,2,1,0:T(8,128)S(1)}, u32[]{:S(2)}, u32[]{:S(2)}) collective-permute-start(f32[4,1,128,128]{3,2,1,0:T(8,128)S(1)} %get-tuple-element.49), channel_id=1, source_target_pairs={{0,4},{4,8},{8,12},{1,5},{5,9},{9,13},{2,6},{6,10},{10,14},{3,7},{... | collective-permute-start | bytes 786440 | tf_op jit(solution)/shard_map/ppermute | solution.py:15
  144.3 3.4 %collective-permute-start.21 = (f32[4,1,128,128]{3,2,1,0:T(8,128)S(1)}, f32[4,1,128,128]{3,2,1,0:T(8,128)S(1)}, u32[]{:S(2)}, u32[]{:S(2)}) collective-permute-start(f32[4,1,128,128]{3,2,1,0:T(8,128)S(1)} %get-tuple-element.50), channel_id=1, source_target_pairs={{4,0},{8,4},{12,8},{5,1},{9,5},{13,9},{6,2},{10,6},{14,10},{7,3},{... | collective-permute-start | bytes 786440 | tf_op jit(solution)/shard_map/ppermute | solution.py:17
  149.3 7.5 %collective-permute-start.24 = (f32[4,1,128,128]{3,2,1,0:T(8,128)S(1)}, f32[4,1,128,128]{3,2,1,0:T(8,128)S(1)}, u32[]{:S(2)}, u32[]{:S(2)}) collective-permute-start(f32[4,1,128,128]{3,2,1,0:T(8,128)S(1)} %get-tuple-element.47), channel_id=1, source_target_pairs={{0,4},{4,8},{8,12},{1,5},{5,9},{9,13},{2,6},{6,10},{10,14},{3,7},{... | collective-permute-start | bytes 786440 | tf_op jit(solution)/shard_map/ppermute | solution.py:15
  155.5 3.4 %collective-permute-start.23 = (f32[4,1,128,128]{3,2,1,0:T(8,128)S(1)}, f32[4,1,128,128]{3,2,1,0:T(8,128)S(1)}, u32[]{:S(2)}, u32[]{:S(2)}) collective-permute-start(f32[4,1,128,128]{3,2,1,0:T(8,128)S(1)} %get-tuple-element.48), channel_id=1, source_target_pairs={{4,0},{8,4},{12,8},{5,1},{9,5},{13,9},{6,2},{10,6},{14,10},{7,3},{... | collective-permute-start | bytes 786440 | tf_op jit(solution)/shard_map/ppermute | solution.py:17
  160.5 7.7 %collective-permute-start.26 = (f32[4,1,128,128]{3,2,1,0:T(8,128)S(1)}, f32[4,1,128,128]{3,2,1,0:T(8,128)S(1)}, u32[]{:S(2)}, u32[]{:S(2)}) collective-permute-start(f32[4,1,128,128]{3,2,1,0:T(8,128)S(1)} %get-tuple-element.45), channel_id=1, source_target_pairs={{0,4},{4,8},{8,12},{1,5},{5,9},{9,13},{2,6},{6,10},{10,14},{3,7},{... | collective-permute-start | bytes 786440 | tf_op jit(solution)/shard_map/ppermute | solution.py:15
  166.6 3.4 %collective-permute-start.25 = (f32[4,1,128,128]{3,2,1,0:T(8,128)S(1)}, f32[4,1,128,128]{3,2,1,0:T(8,128)S(1)}, u32[]{:S(2)}, u32[]{:S(2)}) collective-permute-start(f32[4,1,128,128]{3,2,1,0:T(8,128)S(1)} %get-tuple-element.46), channel_id=1, source_target_pairs={{4,0},{8,4},{12,8},{5,1},{9,5},{13,9},{6,2},{10,6},{14,10},{7,3},{... | collective-permute-start | bytes 786440 | tf_op jit(solution)/shard_map/ppermute | solution.py:17
  171.6 7.5 %collective-permute-start.28 = (f32[4,1,128,128]{3,2,1,0:T(8,128)S(1)}, f32[4,1,128,128]{3,2,1,0:T(8,128)S(1)}, u32[]{:S(2)}, u32[]{:S(2)}) collective-permute-start(f32[4,1,128,128]{3,2,1,0:T(8,128)S(1)} %get-tuple-element.43), channel_id=1, source_target_pairs={{0,4},{4,8},{8,12},{1,5},{5,9},{9,13},{2,6},{6,10},{10,14},{3,7},{... | collective-permute-start | bytes 786440 | tf_op jit(solution)/shard_map/ppermute | solution.py:15
  182.8 7.6 %collective-permute-start.30 = (f32[4,1,128,128]{3,2,1,0:T(8,128)S(1)}, f32[4,1,128,128]{3,2,1,0:T(8,128)S(1)}, u32[]{:S(2)}, u32[]{:S(2)}) collective-permute-start(f32[4,1,128,128]{3,2,1,0:T(8,128)S(1)} %get-tuple-element.41), channel_id=1, source_target_pairs={{0,4},{4,8},{8,12},{1,5},{5,9},{9,13},{2,6},{6,10},{10,14},{3,7},{... | collective-permute-start | bytes 786440 | tf_op jit(solution)/shard_map/ppermute | solution.py:15
  195.6 8.2 %collective-permute-start.32 = (f32[4,1,128,128]{3,2,1,0:T(8,128)}, f32[4,1,128,128]{3,2,1,0:T(8,128)}, u32[]{:S(2)}, u32[]{:S(2)}) collective-permute-start(f32[4,1,128,128]{3,2,1,0:T(8,128)} %get-tuple-element.39), channel_id=1, source_target_pairs={{0,4},{4,8},{8,12},{1,5},{5,9},{9,13},{2,6},{6,10},{10,14},{3,7},{... | collective-permute-start | bytes 786440 | tf_op jit(solution)/shard_map/ppermute | solution.py:15
  202.5 3.8 %collective-permute-start.31 = (f32[4,1,128,128]{3,2,1,0:T(8,128)}, f32[4,1,128,128]{3,2,1,0:T(8,128)}, u32[]{:S(2)}, u32[]{:S(2)}) collective-permute-start(f32[4,1,128,128]{3,2,1,0:T(8,128)} %get-tuple-element.40), channel_id=1, source_target_pairs={{4,0},{8,4},{12,8},{5,1},{9,5},{13,9},{6,2},{10,6},{14,10},{7,3},{... | collective-permute-start | bytes 786440 | tf_op jit(solution)/shard_map/ppermute | solution.py:17
  212.1 25.0 %collective-permute-start.33 = (f32[4,1,128,128]{3,2,1,0:T(8,128)S(1)}, f32[4,1,128,128]{3,2,1,0:T(8,128)S(1)}, u32[]{:S(2)}, u32[]{:S(2)}) collective-permute-start(f32[4,1,128,128]{3,2,1,0:T(8,128)S(1)} %get-tuple-element.38), channel_id=1, source_target_pairs={{4,0},{8,4},{12,8},{5,1},{9,5},{13,9},{6,2},{10,6},{14,10},{7,3},{... | collective-permute-start | bytes 786440 | tf_op jit(solution)/shard_map/ppermute | solution.py:17
  213.4 23.7 %collective-permute-start.34 = (f32[4,1,128,128]{3,2,1,0:T(8,128)S(1)}, f32[4,1,128,128]{3,2,1,0:T(8,128)S(1)}, u32[]{:S(2)}, u32[]{:S(2)}) collective-permute-start(f32[4,1,128,128]{3,2,1,0:T(8,128)S(1)} %get-tuple-element.37), channel_id=1, source_target_pairs={{0,4},{4,8},{8,12},{1,5},{5,9},{9,13},{2,6},{6,10},{10,14},{3,7},{... | collective-permute-start | bytes 786440 | tf_op jit(solution)/shard_map/ppermute | solution.py:15
  (83 other events, 457.4 us)
